TPU v7x, 128 devices: a whole 4x4x4 slice. The times are simulated.
128 devices in a mesh: wide: 32 (over x, y, core), narrow: 4 (over z).
Axes of the slice: x: 4, y: 4, z: 4, core: 2. Of those that a mesh axis runs over, the one named last changes fastest.
Arguments:
- raw_samples: bfloat16 [1024, 32, 16384], P(('wide', 'narrow')), as said below
- filter_taps: float32 [64], replicated, may hold values from -0.75 to 0.75
- tile_pairs: int32 [16, 2], replicated, may hold values from 0 to 127, as said below
- tile_owners: int32 [16], replicated, may hold values from 0 to 3, as said below
Outputs:
- correlation_stacks: float32 [32, 64, 512], P('narrow', 'wide')
Inputs may be any that keep to these rules, and one draw needn't show every extreme that they name: `raw_samples`: noise samples, scaled per channel and per window. `tile_pairs`: each row is (source block, receiver block), and the two blocks differ. `tile_owners`: each owner has at most 8 tiles, and some owner has exactly 8.
All inputs are finite; a program needn't handle non-finite values.
Results may differ from a plain program's by a relative error of at most 0.0074.
Values may be sent and summed in bfloat16 or wider, within the bound.
No kernel may reach another device: no remote copies, remote signals or barrier semaphores. Data moves between devices by JAX's collectives and lax.ppermute only.
A program may use at most 128 MiB of HBM per device.

v0:
```python
import math
import jax
import jax.numpy as jnp
from jax import lax
from jax.sharding import PartitionSpec as P

NFFT = 4096
DECIM = 4
NBINS = 1024
SMOOTH = 63
LAGS = 512
BLK = 8
SLOTS = 8
water_level = 0.2
epsilon = 1e-06


def fir_tables(filter_taps, block_size):
    in_rows = jnp.arange(DECIM * block_size, dtype=jnp.int32)[:, None]
    out_cols = jnp.arange(block_size, dtype=jnp.int32)[None, :]
    this_index = DECIM * out_cols + DECIM - 1 - in_rows
    last_index = this_index + DECIM * block_size
    tap_count = filter_taps.shape[0]

    def taps_at(tap_index):
        inside = (tap_index >= 0) & (tap_index < tap_count)
        values = jnp.take(filter_taps, jnp.clip(tap_index, 0, tap_count - 1))
        return jnp.where(inside, values, jnp.zeros_like(values)).astype(jnp.bfloat16)

    return (taps_at(this_index), taps_at(last_index))


def decimate(samples, filter_taps):
    row_count, row_length = samples.shape
    block_size = min(128, row_length // DECIM)
    this_table, last_table = fir_tables(filter_taps, block_size)
    segments = samples.reshape(-1, DECIM * block_size)
    current = jnp.dot(segments, this_table, preferred_element_type=jnp.float32).reshape(
        row_count, -1, block_size
    )
    spilled = jnp.dot(segments, last_table, preferred_element_type=jnp.float32).reshape(
        row_count, -1, block_size
    )
    spilled = jnp.pad(spilled[:, :-1], ((0, 0), (1, 0), (0, 0)))
    return (current + spilled).reshape(row_count, -1).astype(jnp.bfloat16)


def dft_table(point_count, bin_count):
    sample_index = jnp.arange(point_count, dtype=jnp.int32)[:, None]
    frequency = 1 + jnp.arange(bin_count, dtype=jnp.int32)[None, :]
    angle = (sample_index * frequency % point_count).astype(jnp.float32) * (
        2.0 * math.pi / point_count
    )
    return jnp.concatenate([jnp.cos(angle), -jnp.sin(angle)], axis=1).astype(jnp.bfloat16)


def lag_table(point_count, bin_count, lag_count, window_count):
    frequency = 1 + jnp.arange(bin_count, dtype=jnp.int32)[:, None]
    shifted = jnp.arange(lag_count, dtype=jnp.int32)[None, :] - lag_count // 2 + point_count
    angle = (frequency * shifted % point_count).astype(jnp.float32) * (2.0 * math.pi / point_count)
    weight = 1.0 / math.sqrt(window_count * bin_count)
    return jnp.concatenate([jnp.cos(angle) * weight, -jnp.sin(angle) * weight], axis=0)


def smoother(bin_count, span_width):
    bin_index = jnp.arange(bin_count, dtype=jnp.int32)
    nearby = (jnp.abs(bin_index[:, None] - bin_index[None, :]) <= (span_width - 1) // 2).astype(
        jnp.float32
    )
    return nearby / jnp.sum(nearby, axis=0, keepdims=True)


def whiten(decimated):
    spectrum = jnp.dot(
        decimated, dft_table(decimated.shape[1], NBINS), preferred_element_type=jnp.float32
    )
    real_part = spectrum[:, :NBINS]
    imag_part = spectrum[:, NBINS:]
    magnitude = jnp.sqrt(real_part * real_part + imag_part * imag_part)
    smooth = jnp.dot(magnitude, smoother(NBINS, SMOOTH), precision=lax.Precision.HIGHEST)
    floor_level = water_level * jnp.mean(smooth, axis=1, keepdims=True) + epsilon
    factor = 1.0 / (smooth + floor_level)
    return (spectrum * jnp.concatenate([factor, factor], axis=1)).astype(jnp.bfloat16)


def block_start(block_index, chan_dev, wide_count, narrow_count):
    first_channel = block_index * BLK
    shard_index = first_channel // chan_dev
    return (
        shard_index % narrow_count * wide_count + shard_index // narrow_count
    ) * chan_dev + first_channel % chan_dev


def gather_rows(spectra, starts):

    def one_block(start_row):
        return lax.dynamic_slice_in_dim(spectra, start_row, BLK, 0)

    return jax.vmap(one_block)(starts)


def slot_cross(source, target, live_slots):
    highest = lax.Precision.HIGHEST
    src_real = source[..., :NBINS]
    src_imag = source[..., NBINS:]
    dst_real = target[..., :NBINS]
    dst_imag = target[..., NBINS:]
    real_sum = jnp.einsum("siwf,sjwf->ijsf", src_real, dst_real, precision=highest) + jnp.einsum(
        "siwf,sjwf->ijsf", src_imag, dst_imag, precision=highest
    )
    imag_sum = jnp.einsum("siwf,sjwf->ijsf", src_real, dst_imag, precision=highest) - jnp.einsum(
        "siwf,sjwf->ijsf", src_imag, dst_real, precision=highest
    )
    slot_count = source.shape[0]
    merged = jnp.concatenate(
        [
            real_sum.reshape(BLK * BLK, slot_count, NBINS),
            imag_sum.reshape(BLK * BLK, slot_count, NBINS),
        ],
        axis=2,
    )
    return merged * live_slots[None, :, None]


def stack_pairs(partial_value, window_count, wide_count):
    lag_basis = lag_table(NFFT, NBINS, LAGS, window_count)
    slot_count = partial_value.shape[1]
    pair_share = partial_value.shape[0] // wide_count
    summed = lax.psum_scatter(partial_value, "wide", scatter_dimension=0, tiled=True)
    flat = summed.reshape(pair_share * slot_count, 2 * NBINS)
    return jnp.dot(flat, lag_basis, precision=lax.Precision.HIGHEST).reshape(
        pair_share, slot_count, LAGS
    )


def on_device(raw_samples, filter_taps, tile_pairs, tile_owners):
    wide_count = lax.axis_size("wide")
    narrow_count = lax.axis_size("narrow")
    chan_dev = raw_samples.shape[0]
    window_total = raw_samples.shape[1]
    arrived = lax.all_to_all(raw_samples, "wide", split_axis=1, concat_axis=0, tiled=True)
    flat_rows = arrived.reshape(-1, arrived.shape[2])
    whitened = whiten(decimate(flat_rows, filter_taps)).reshape(
        arrived.shape[0], arrived.shape[1], 2 * NBINS
    )
    owner_index = lax.axis_index("narrow")
    slot_ids = jnp.arange(SLOTS, dtype=jnp.int32)
    owner_ids = jnp.arange(narrow_count, dtype=jnp.int32)
    owned_all = tile_owners[None, :] == owner_ids[:, None]
    rank_all = jnp.cumsum(owned_all.astype(jnp.int32), axis=1) - 1
    select_all = owned_all[:, None, :] & (rank_all[:, None, :] == slot_ids[None, :, None])
    select = lax.dynamic_index_in_dim(select_all, owner_index, 0, keepdims=False)
    pick_all = select_all.astype(jnp.int32)
    chosen_all = jnp.sum(pick_all[:, :, :, None] * tile_pairs[None, None, :, :], axis=2)
    chosen = lax.dynamic_index_in_dim(chosen_all, owner_index, 0, keepdims=False)
    live_slots = jnp.sum(select.astype(jnp.int32), axis=1).astype(jnp.float32)
    spectra = lax.all_gather(whitened, "narrow", axis=0, tiled=True)
    source = gather_rows(
        spectra, block_start(chosen[:, 0], chan_dev, wide_count, narrow_count)
    ).astype(jnp.float32)
    target = gather_rows(
        spectra, block_start(chosen[:, 1], chan_dev, wide_count, narrow_count)
    ).astype(jnp.float32)
    partial_value = slot_cross(source, target, live_slots)
    stacked = jnp.transpose(stack_pairs(partial_value, window_total, wide_count), (1, 0, 2))
    return stacked


def solution(mesh):
    in_specs = (P(("wide", "narrow"), None, None), P(), P(), P())
    out_specs = P("narrow", "wide", None)
    return jax.shard_map(
        on_device, mesh=mesh, in_specs=in_specs, out_specs=out_specs, check_vma=False
    )
```

profile of v0, /device:TPU:0, one launch (start us, length us, event | category | flops | bytes accessed | tf_op | source)
XLA Modules:
  0.0 474.6 jit_solution(13282219317979138211)
XLA Ops:
  6.5 11.2 %copy.33 = bf16[8,32,16384]{2,0,1:T(8,128)(2,1)} copy(bf16[8,32,16384]{2,1,0:T(8,128)(2,1)} %param.6) | data formatting | bytes 16777216 | tf_op args[0]
  17.7 7.7 %all-to-all-start = ((bf16[8,32,16384]{2,0,1:T(8,128)(2,1)}), bf16[8,32,16384]{2,0,1:T(8,128)(2,1)}, u32[]{:S(2)}, u32[]{:S(2)}) async-start(bf16[8,32,16384]{2,0,1:T(8,128)(2,1)} %copy.33), calls=%async_computation | async-start | bytes 16777216 | tf_op jit(solution)/shard_map/all_to_all | solution.py:141
  28.8 69.1 %cosine_convert_fusion = (bf16[4096,1024]{1,0:T(8,128)(2,1)}, bf16[4096,1024]{1,0:T(8,128)(2,1)}) fusion(s32[1024]{0:T(1024)S(1)} %iota_add_fusion), kind=kLoop, calls=%fused_computation.15 | loop fusion | flops 71303168 | bytes 16781312 | tf_op jit(solution)/shard_map/convert.24
  97.9 41.1 %all-to-all-done = bf16[8,32,16384]{2,0,1:T(8,128)(2,1)} async-done(((bf16[8,32,16384]{2,0,1:T(8,128)(2,1)}), bf16[8,32,16384]{2,0,1:T(8,128)(2,1)}, u32[]{:S(2)}, u32[]{:S(2)}) %all-to-all-start) | async-done | bytes 8388640 | tf_op jit(solution)/shard_map/all_to_all | solution.py:141
  138.9 13.5 %reshape_reshape.3 = bf16[8192,512]{1,0:T(8,128)(2,1)} reshape(bf16[32,8,1,16384]{3,1,0,2:T(8,128)(2,1)} %bitcast.65) | data formatting | bytes 16777216 | tf_op jit(solution)/shard_map/reshape;reshape | solution.py:37
  152.4 50.3 %convolution_bitcast_fusion = f32[8192,128]{0,1:T(8,128)} fusion(bf16[8192,512]{1,0:T(8,128)(2,1)} %reshape_reshape.3, bf16[]{:T(256)} %bitcast.63, bf16[]{:T(256)} %bitcast.62, bf16[]{:T(256)} %bitcast.61, bf16[]{:T(256)} %bitcast.60, bf16[]{:T(256)} %bitcast.59, bf16[]{:T(256)} %bitcast.58, bf16[]{:T(256)} %bitcast.57, bf16[]{:T(256)} %bitcast.56, ...), kind=kOutput, calls=%fused_computation.19 | convolution fusion | flops 1082916864 | bytes 12583552 | tf_op jit(solution)/shard_map/dot_general | solution.py:41
  202.7 45.8 %convolution_bitcast_fusion.1 = f32[8192,128]{0,1:T(8,128)} fusion(bf16[8192,512]{1,0:T(8,128)(2,1)S(1)} %bitcast.200, bf16[]{:T(256)} %bitcast.63, bf16[]{:T(256)} %bitcast.62, bf16[]{:T(256)} %bitcast.61, bf16[]{:T(256)} %bitcast.60, bf16[]{:T(256)} %bitcast.59, bf16[]{:T(256)} %bitcast.58, bf16[]{:T(256)} %bitcast.57, bf16[]{:T(256)} %bitcast.56, ...), kind=kOutput, calls=%fused_computation.20 | convolution fusion | flops 1082851328 | bytes 12583552 | tf_op jit(solution)/shard_map/dot_general | solution.py:38
  248.5 5.6 %copy.35 = f32[8192,128]{1,0:T(8,128)} copy(f32[8192,128]{0,1:T(8,128)} %convolution_bitcast_fusion) | data formatting | bytes 8388608 | tf_op jit(solution)/shard_map/dot_general | solution.py:41
  254.1 5.6 %copy.34 = f32[8192,128]{1,0:T(8,128)} copy(f32[8192,128]{0,1:T(8,128)} %convolution_bitcast_fusion.1) | data formatting | bytes 8388608 | tf_op jit(solution)/shard_map/dot_general | solution.py:38
  259.7 4.2 add_convert_fusion
  263.9 2.8 copy.36
  266.7 10.9 %fusion.3 = f32[256,2048]{1,0:T(8,128)S(1)} fusion(bf16[256,4096]{0,1:T(8,128)(2,1)} %bitcast.203, bf16[4096,1024]{1,0:T(8,128)(2,1)} %get-tuple-element.55, bf16[4096,1024]{1,0:T(8,128)(2,1)} %get-tuple-element.54), kind=kOutput, calls=%fused_computation.10 | convolution fusion | flops 4328521728 | bytes 20971520 | tf_op jit(solution)/shard_map/dot_general | solution.py:74
  277.6 3.8 fusion.583
  283.7 57.0 %all-gather.3.cloned.1.call-done = bf16[1024,2048]{1,0:T(8,128)(2,1)} async-done(((bf16[256,2048]{1,0:T(8,128)(2,1)}), bf16[1024,2048]{1,0:T(8,128)(2,1)}) %all-gather.3.cloned.1.call-update) | async-done | bytes 4194320 | tf_op jit(solution)/shard_map/all_gather | solution.py:157
  340.7 18.2 %while.2 = (s32[]{:T(128)}, bf16[1024,1,2048]{2,0,1:T(8,128)(2,1)}, s32[8,3]{0,1:T(4,128)S(1)}, bf16[8,8,1,2048]{3,1,2,0:T(8,128)(2,1)S(1)}, s32[]{:T(128)}) while((s32[]{:T(128)}, bf16[1024,1,2048]{2,0,1:T(8,128)(2,1)}, s32[8,3]{0,1:T(4,128)S(1)}, bf16[8,8,1,2048]{3,1,2,0:T(8,128)(2,1)S(1)}, s32[]{:T(128)}) %tuple.109), condition=%wide.while_cond, body=%wide.while_body.sunk | while | flops 2 | bytes 65641 | solution.py:97
  341.6 1.5 bitcast_dynamic-update-slice_fusion.4
  343.9 1.5 bitcast_dynamic-update-slice_fusion.4
  346.1 1.5 bitcast_dynamic-update-slice_fusion.4
  348.4 1.5 bitcast_dynamic-update-slice_fusion.4
  350.6 1.5 bitcast_dynamic-update-slice_fusion.4
  352.8 1.5 bitcast_dynamic-update-slice_fusion.4
  355.1 1.5 bitcast_dynamic-update-slice_fusion.4
  357.3 1.5 bitcast_dynamic-update-slice_fusion.4
  359.3 17.9 %while.3 = (s32[]{:T(128)}, bf16[1024,1,2048]{2,0,1:T(8,128)(2,1)}, s32[8,3]{0,1:T(4,128)S(1)}, bf16[8,8,1,2048]{3,1,2,0:T(8,128)(2,1)S(1)}, s32[]{:T(128)}) while((s32[]{:T(128)}, bf16[1024,1,2048]{2,0,1:T(8,128)(2,1)}, s32[8,3]{0,1:T(4,128)S(1)}, bf16[8,8,1,2048]{3,1,2,0:T(8,128)(2,1)S(1)}, s32[]{:T(128)}) %tuple.110), condition=%wide.while_cond.1, body=%wide.while_body.1.sunk | while | flops 2 | bytes 65641 | solution.py:97
  360.0 1.5 bitcast_dynamic-update-slice_fusion.5
  362.2 1.5 bitcast_dynamic-update-slice_fusion.5
  364.4 1.5 bitcast_dynamic-update-slice_fusion.5
  366.7 1.5 bitcast_dynamic-update-slice_fusion.5
  378.1 2.6 maximum_multiply_fusion
  380.8 9.7 %cosine_multiply_fusion = (f32[1024,512]{1,0:T(8,128)S(1)}, f32[1024,512]{1,0:T(8,128)}) fusion(s32[512]{0:T(512)S(1)} %iota_add_fusion.1, s32[1024]{0:T(1024)S(1)} %iota_add_fusion), kind=kLoop, calls=%fused_computation.42 | loop fusion | flops 8912896 | bytes 4200448 | tf_op jit(solution)/shard_map/mul | solution.py:62
  390.5 72.8 %reduce-scatter.2.cloned.1.call-done = f32[2,8,2048]{2,1,0:T(8,128)} async-done(((f32[64,8,2048]{2,1,0:T(8,128)}), f32[2,8,2048]{2,1,0:T(8,128)}) %reduce-scatter.2.cloned.1.call-update) | async-done | bytes 131088 | tf_op jit(solution)/shard_map/reduce_scatter | solution.py:129
  463.3 3.8 fusion.20
  (83 shorter events, 24.4 us)
Async XLA Ops:
  17.7 8.1 %copy-start = (f32[64]{0:T(128)S(1)}, f32[64]{0:T(128)}, u32[]{:S(2)}) copy-start(f32[64]{0:T(128)} %param.7) | copy-start | bytes 772
  17.7 121.2 %all-to-all-start = ((bf16[8,32,16384]{2,0,1:T(8,128)(2,1)}), bf16[8,32,16384]{2,0,1:T(8,128)(2,1)}, u32[]{:S(2)}, u32[]{:S(2)}) async-start(bf16[8,32,16384]{2,0,1:T(8,128)(2,1)} %copy.33), calls=%async_computation | async-start | bytes 16777216 | tf_op jit(solution)/shard_map/all_to_all | solution.py:141
  25.4 315.2 %all-gather.3.cloned.1.call-start = ((), (), s32[]{:S(2)}) async-start(), calls=%async_computation.3 | async-start | bytes 5242880 | tf_op jit(solution)/shard_map/all_gather | solution.py:157
  152.4 50.3 %slice-start = ((s8[8388608]{0:T(1024)(128)(4,1)}), s8[4194304]{0:T(1024)(128)(4,1)S(1)}, s32[]{:S(2)}) async-start(s8[8388608]{0:T(1024)(128)(4,1)} %bitcast.199), calls=%async_computation.4 | async-start | bytes 8388608
  152.4 50.3 %slice-start.1 = ((s8[8388608]{0:T(1024)(128)(4,1)}), s8[4194304]{0:T(1024)(128)(4,1)S(1)}, s32[]{:S(2)}) async-start(s8[8388608]{0:T(1024)(128)(4,1)} %bitcast.199), calls=%async_computation.5 | async-start | bytes 8388608
  281.4 1.6 copy-start.2
  281.4 1.8 copy-start.1
  283.0 180.3 %reduce-scatter.2.cloned.1.call-start = ((), (), s32[]{:S(2)}) async-start(), calls=%async_computation.2 | async-start | bytes 4325376 | tf_op jit(solution)/shard_map/reduce_scatter | solution.py:129
Sparse Core Ops, SparseCore 0:
  283.1 57.5 all-gather.2
  380.9 82.3 reduce-scatter.1
where the time goes:
time: 477 us; the launch traced here: 475 us
  waiting for transfers between devices  171 us (36%)
  matrix products  115 us (24%)
  other arithmetic  88.6 us (19%)
  local copies, waits for them, and re-layouts  78.4 us (16%)
  between operations  13.6 us (3%)
  starting transfers between devices  7.96 us (2%)
    reduce_scatter x1, waiting for transfers between devices, stack_pairs(): lax.psum_scatter(partial_value, 'wide', scatter_dimension=0, tiled=True)  72.8 us
    another operation x3, other arithmetic  69.2 us
    all_gather x1, waiting for transfers between devices, on_device(): spectra = lax.all_gather(whitened, 'narrow', axis=0, tiled=True)  57 us
    dot_general x1, matrix products, decimate(): jnp.dot(segments, last_table, preferred_element_type=jnp.float32)  50.3 us
    dot_general x1, matrix products, decimate(): jnp.dot(segments, this_table, preferred_element_type=jnp.float32)  45.8 us
    all_to_all x1, waiting for transfers between devices, on_device(): lax.all_to_all(raw_samples, 'wide', split_axis=1, concat_axis=0, tiled=True)  41.1 us
    gather x48, local copies, waits for them, and re-layouts  35.5 us
    another operation x1, local copies, waits for them, and re-layouts, decimate(): segments = samples.reshape(-1, DECIM * block_size)  13.5 us
  transfers between devices with their start and end apart: 3, of which 3 were waited for; matrix products, arithmetic and copies ran while one was open for 17% of the time, Pallas kernels for 0%

commit v1 on v0

--- a/solution.py
+++ b/solution.py
@@ -154,7 +154,9 @@
     chosen_all = jnp.sum(pick_all[:, :, :, None] * tile_pairs[None, None, :, :], axis=2)
     chosen = lax.dynamic_index_in_dim(chosen_all, owner_index, 0, keepdims=False)
     live_slots = jnp.sum(select.astype(jnp.int32), axis=1).astype(jnp.float32)
-    spectra = lax.all_gather(whitened, "narrow", axis=0, tiled=True)
+    spectra = jnp.concatenate(
+        lax.all_to_all(jnp.stack([whitened] * lax.axis_size("narrow")), "narrow", 0, 0), axis=0
+    )
     source = gather_rows(
         spectra, block_start(chosen[:, 0], chan_dev, wide_count, narrow_count)
     ).astype(jnp.float32)

time: 477 us -> 483 us (1.013)
  starting transfers between devices: 7.96 us -> 13.3 us
    all_gather x1 -> x0, waiting for transfers between devices: 57 us -> none  [on_device(): spectra = lax.all_gather(whitened, 'narrow', axis=0, tiled=True)]
    all_to_all x0 -> x1, waiting for transfers between devices: none -> 39.6 us  [on_device(): lax.all_to_all(jnp.stack([whitened] * lax.axis_size('narrow')), 'narrow',...]
    reduce_scatter x1, waiting for transfers between devices: 72.8 us -> 91.8 us  [stack_pairs(): lax.psum_scatter(partial_value, 'wide', scatter_dimension=0, tiled=True)]
    all_to_all x0 -> x1, starting transfers between devices: none -> 5.44 us  [on_device(): lax.all_to_all(jnp.stack([whitened] * lax.axis_size('narrow')), 'narrow',...]
where the time goes in v1:
time: 483 us; the launch traced here: 480 us
  waiting for transfers between devices  173 us (36%)
  matrix products  114 us (24%)
  other arithmetic  87.7 us (18%)
  local copies, waits for them, and re-layouts  77.8 us (16%)
  between operations  13.6 us (3%)
  starting transfers between devices  13.3 us (3%)
    reduce_scatter x1, waiting for transfers between devices, stack_pairs(): lax.psum_scatter(partial_value, 'wide', scatter_dimension=0, tiled=True)  91.8 us
    another operation x3, other arithmetic  69.2 us
    dot_general x1, matrix products, decimate(): jnp.dot(segments, last_table, preferred_element_type=jnp.float32)  50.2 us
    dot_general x1, matrix products, decimate(): jnp.dot(segments, this_table, preferred_element_type=jnp.float32)  45.7 us
    all_to_all x1, waiting for transfers between devices, on_device(): lax.all_to_all(raw_samples, 'wide', split_axis=1, concat_axis=0, tiled=True)  41.4 us
    all_to_all x1, waiting for transfers between devices, on_device(): lax.all_to_all(jnp.stack([whitened] * lax.axis_size('narrow')), 'narrow',...  39.6 us
    gather x48, local copies, waits for them, and re-layouts  32.5 us
    another operation x1, local copies, waits for them, and re-layouts, decimate(): segments = samples.reshape(-1, DECIM * block_size)  13.5 us
  transfers between devices with their start and end apart: 3, of which 3 were waited for; matrix products, arithmetic and copies ran while one was open for 17% of the time, Pallas kernels for 0%

profile of v1, /device:TPU:0, one launch (start us, length us, event | category | flops | bytes accessed | tf_op | source)
XLA Modules:
  0.0 480.1 jit_solution(7911864843544485034)
XLA Ops:
  6.5 11.2 %copy.31 = bf16[8,32,16384]{2,0,1:T(8,128)(2,1)} copy(bf16[8,32,16384]{2,1,0:T(8,128)(2,1)} %param.6) | data formatting | bytes 16777216 | tf_op args[0]
  17.7 7.9 %all-to-all-start = ((bf16[8,32,16384]{2,0,1:T(8,128)(2,1)}), bf16[8,32,16384]{2,0,1:T(8,128)(2,1)}, u32[]{:S(2)}, u32[]{:S(2)}) async-start(bf16[8,32,16384]{2,0,1:T(8,128)(2,1)} %copy.31), calls=%async_computation | async-start | bytes 16777216 | tf_op jit(solution)/shard_map/all_to_all | solution.py:141
  28.7 69.1 %cosine_convert_fusion = (bf16[4096,1024]{1,0:T(8,128)(2,1)}, bf16[4096,1024]{1,0:T(8,128)(2,1)}) fusion(s32[1024]{0:T(1024)S(1)} %iota_add_fusion), kind=kLoop, calls=%fused_computation.15 | loop fusion | flops 71303168 | bytes 16781312 | tf_op jit(solution)/shard_map/convert.24
  97.8 41.4 %all-to-all-done = bf16[8,32,16384]{2,0,1:T(8,128)(2,1)} async-done(((bf16[8,32,16384]{2,0,1:T(8,128)(2,1)}), bf16[8,32,16384]{2,0,1:T(8,128)(2,1)}, u32[]{:S(2)}, u32[]{:S(2)}) %all-to-all-start) | async-done | bytes 8388640 | tf_op jit(solution)/shard_map/all_to_all | solution.py:141
  139.2 13.5 %reshape_reshape.3 = bf16[8192,512]{1,0:T(8,128)(2,1)} reshape(bf16[32,8,1,16384]{3,1,0,2:T(8,128)(2,1)} %bitcast.65) | data formatting | bytes 16777216 | tf_op jit(solution)/shard_map/reshape;reshape | solution.py:37
  152.6 50.2 %convolution_bitcast_fusion = f32[8192,128]{0,1:T(8,128)} fusion(bf16[8192,512]{1,0:T(8,128)(2,1)} %reshape_reshape.3, bf16[]{:T(256)} %bitcast.63, bf16[]{:T(256)} %bitcast.62, bf16[]{:T(256)} %bitcast.61, bf16[]{:T(256)} %bitcast.60, bf16[]{:T(256)} %bitcast.59, bf16[]{:T(256)} %bitcast.58, bf16[]{:T(256)} %bitcast.57, bf16[]{:T(256)} %bitcast.56, ...), kind=kOutput, calls=%fused_computation.19 | convolution fusion | flops 1082916864 | bytes 12583552 | tf_op jit(solution)/shard_map/dot_general | solution.py:41
  202.8 45.7 %convolution_bitcast_fusion.1 = f32[8192,128]{0,1:T(8,128)} fusion(bf16[8192,512]{1,0:T(8,128)(2,1)S(1)} %bitcast.200, bf16[]{:T(256)} %bitcast.63, bf16[]{:T(256)} %bitcast.62, bf16[]{:T(256)} %bitcast.61, bf16[]{:T(256)} %bitcast.60, bf16[]{:T(256)} %bitcast.59, bf16[]{:T(256)} %bitcast.58, bf16[]{:T(256)} %bitcast.57, bf16[]{:T(256)} %bitcast.56, ...), kind=kOutput, calls=%fused_computation.20 | convolution fusion | flops 1082851328 | bytes 12583552 | tf_op jit(solution)/shard_map/dot_general | solution.py:38
  248.5 5.6 %copy.33 = f32[8192,128]{1,0:T(8,128)} copy(f32[8192,128]{0,1:T(8,128)} %convolution_bitcast_fusion) | data formatting | bytes 8388608 | tf_op jit(solution)/shard_map/dot_general | solution.py:41
  254.1 5.6 %copy.32 = f32[8192,128]{1,0:T(8,128)} copy(f32[8192,128]{0,1:T(8,128)} %convolution_bitcast_fusion.1) | data formatting | bytes 8388608 | tf_op jit(solution)/shard_map/dot_general | solution.py:38
  259.7 4.2 add_convert_fusion
  263.9 2.7 copy.34
  266.6 10.9 %fusion.3 = f32[256,2048]{1,0:T(8,128)S(1)} fusion(bf16[256,4096]{0,1:T(8,128)(2,1)} %bitcast.203, bf16[4096,1024]{1,0:T(8,128)(2,1)} %get-tuple-element.47, bf16[4096,1024]{1,0:T(8,128)(2,1)} %get-tuple-element.46), kind=kOutput, calls=%fused_computation.10 | convolution fusion | flops 4328521728 | bytes 20971520 | tf_op jit(solution)/shard_map/dot_general | solution.py:74
  277.5 3.8 fusion.583
  281.9 2.5 stack.3
  284.5 5.4 %all-to-all-start.1 = ((bf16[4,256,1,2048]{3,1,2,0:T(8,128)(2,1)}), bf16[4,256,1,2048]{3,1,2,0:T(8,128)(2,1)}, u32[]{:S(2)}, u32[]{:S(2)}) async-start(bf16[4,256,1,2048]{3,1,2,0:T(8,128)(2,1)} %stack.3), calls=%async_computation.1 | async-start | bytes 8388608 | tf_op jit(solution)/shard_map/all_to_all | solution.py:158
  290.5 39.6 %all-to-all-done.1 = bf16[4,256,1,2048]{3,1,2,0:T(8,128)(2,1)} async-done(((bf16[4,256,1,2048]{3,1,2,0:T(8,128)(2,1)}), bf16[4,256,1,2048]{3,1,2,0:T(8,128)(2,1)}, u32[]{:S(2)}, u32[]{:S(2)}) %all-to-all-start.1) | async-done | bytes 4194336 | tf_op jit(solution)/shard_map/all_to_all | solution.py:158
  330.2 16.7 %while.2 = (s32[]{:T(128)}, bf16[1024,1,2048]{2,0,1:T(8,128)(2,1)}, s32[8,3]{0,1:T(4,128)S(1)}, bf16[8,8,1,2048]{3,1,2,0:T(8,128)(2,1)S(1)}, s32[]{:T(128)}) while((s32[]{:T(128)}, bf16[1024,1,2048]{2,0,1:T(8,128)(2,1)}, s32[8,3]{0,1:T(4,128)S(1)}, bf16[8,8,1,2048]{3,1,2,0:T(8,128)(2,1)S(1)}, s32[]{:T(128)}) %tuple.100), condition=%wide.while_cond, body=%wide.while_body.sunk | while | flops 2 | bytes 65641 | solution.py:97
  331.1 1.4 bitcast_dynamic-update-slice_fusion.4
  333.1 1.4 bitcast_dynamic-update-slice_fusion.4
  335.2 1.4 bitcast_dynamic-update-slice_fusion.4
  337.2 1.4 bitcast_dynamic-update-slice_fusion.4
  339.3 1.4 bitcast_dynamic-update-slice_fusion.4
  343.4 1.4 bitcast_dynamic-update-slice_fusion.4
  347.3 16.4 %while.3 = (s32[]{:T(128)}, bf16[1024,1,2048]{2,0,1:T(8,128)(2,1)}, s32[8,3]{0,1:T(4,128)S(1)}, bf16[8,8,1,2048]{3,1,2,0:T(8,128)(2,1)S(1)}, s32[]{:T(128)}) while((s32[]{:T(128)}, bf16[1024,1,2048]{2,0,1:T(8,128)(2,1)}, s32[8,3]{0,1:T(4,128)S(1)}, bf16[8,8,1,2048]{3,1,2,0:T(8,128)(2,1)S(1)}, s32[]{:T(128)}) %tuple.97), condition=%wide.while_cond.1, body=%wide.while_body.1.sunk | while | flops 2 | bytes 65641 | solution.py:97
  349.9 1.4 bitcast_dynamic-update-slice_fusion.5
  352.0 1.4 bitcast_dynamic-update-slice_fusion.5
  356.1 1.4 bitcast_dynamic-update-slice_fusion.5
  362.2 1.4 bitcast_dynamic-update-slice_fusion.5
  364.6 2.6 maximum_multiply_fusion
  367.3 9.7 %cosine_multiply_fusion = (f32[1024,512]{1,0:T(8,128)S(1)}, f32[1024,512]{1,0:T(8,128)}) fusion(s32[512]{0:T(512)S(1)} %iota_add_fusion.1, s32[1024]{0:T(1024)S(1)} %iota_add_fusion), kind=kLoop, calls=%fused_computation.42 | loop fusion | flops 8912896 | bytes 4200448 | tf_op jit(solution)/shard_map/mul | solution.py:62
  377.0 91.8 %reduce-scatter.2.cloned.1.call-done = f32[2,8,2048]{2,1,0:T(8,128)} async-done(((f32[64,8,2048]{2,1,0:T(8,128)}), f32[2,8,2048]{2,1,0:T(8,128)}) %reduce-scatter.2.cloned.1.call-update) | async-done | bytes 131088 | tf_op jit(solution)/shard_map/reduce_scatter | solution.py:129
  468.8 3.8 fusion.20
  (83 shorter events, 24.4 us)
Async XLA Ops:
  17.7 8.1 %copy-start = (f32[64]{0:T(128)S(1)}, f32[64]{0:T(128)}, u32[]{:S(2)}) copy-start(f32[64]{0:T(128)} %param.7) | copy-start | bytes 772
  17.7 121.4 %all-to-all-start = ((bf16[8,32,16384]{2,0,1:T(8,128)(2,1)}), bf16[8,32,16384]{2,0,1:T(8,128)(2,1)}, u32[]{:S(2)}, u32[]{:S(2)}) async-start(bf16[8,32,16384]{2,0,1:T(8,128)(2,1)} %copy.31), calls=%async_computation | async-start | bytes 16777216 | tf_op jit(solution)/shard_map/all_to_all | solution.py:141
  152.6 50.2 %slice-start = ((s8[8388608]{0:T(1024)(128)(4,1)}), s8[4194304]{0:T(1024)(128)(4,1)S(1)}, s32[]{:S(2)}) async-start(s8[8388608]{0:T(1024)(128)(4,1)} %bitcast.199), calls=%async_computation.4 | async-start | bytes 8388608
  152.6 50.2 %slice-start.1 = ((s8[8388608]{0:T(1024)(128)(4,1)}), s8[4194304]{0:T(1024)(128)(4,1)S(1)}, s32[]{:S(2)}) async-start(s8[8388608]{0:T(1024)(128)(4,1)} %bitcast.199), calls=%async_computation.5 | async-start | bytes 8388608
  284.5 5.4 %copy-start.2 = (s32[16]{0:T(128)S(1)}, s32[16]{0:T(128)}, u32[]{:S(2)}) copy-start(s32[16]{0:T(128)} %param.9) | copy-start | bytes 196
  284.5 5.7 %copy-start.1 = (s32[16,2]{0,1:T(2,128)S(1)}, s32[16,2]{0,1:T(2,128)}, u32[]{:S(2)}) copy-start(s32[16,2]{0,1:T(2,128)} %param.8) | copy-start | bytes 388
  284.5 45.7 %all-to-all-start.1 = ((bf16[4,256,1,2048]{3,1,2,0:T(8,128)(2,1)}), bf16[4,256,1,2048]{3,1,2,0:T(8,128)(2,1)}, u32[]{:S(2)}, u32[]{:S(2)}) async-start(bf16[4,256,1,2048]{3,1,2,0:T(8,128)(2,1)} %stack.3), calls=%async_computation.1 | async-start | bytes 8388608 | tf_op jit(solution)/shard_map/all_to_all | solution.py:158
  289.9 178.9 %reduce-scatter.2.cloned.1.call-start = ((), (), s32[]{:S(2)}) async-start(), calls=%async_computation.3 | async-start | bytes 4325376 | tf_op jit(solution)/shard_map/reduce_scatter | solution.py:129
Sparse Core Ops, SparseCore 0:
  367.4 101.3 reduce-scatter.1
